TPU v7x, 128 devices: a whole 4x4x4 slice. The times are simulated.
128 devices in a mesh: row: 16 (over z_lo, x, core), col: 8 (over y, z_hi).
Axes of the slice: x: 4, y: 4, z: 4 (z_hi: 2, z_lo: 2; z = z_hi * 2 + z_lo), core: 2. Of those that a mesh axis runs over, the one named last changes fastest.
Arguments:
- shared_rows: float32 [2048, 16384], P('row', 'col'), may hold values from -0.125 to 0.125
- event_counts: int32 [16], replicated, may hold values from 32 to 128, as said below
- ridge: float32 [16384], P('col'), may hold values from 0.5 to 2
- items: float32 [1024, 16384], P('row', 'col'), may hold values from -6 to 6
- cand_ids: int32 [512], replicated, may hold values from 0 to 1023
- theta: float32 [16384], P('col'), may hold values from -0.046875 to 0.046875
Outputs:
- gram_tile: float32 [16384, 16384], P('row', 'col')
- scores: float32 [512], replicated
Inputs may be any that keep to these rules, and one draw needn't show every extreme that they name: event_counts[s] counts the live slots at the start of row shard s's 128 slots; some shard is full.
All inputs are finite; a program needn't handle non-finite values.
Results may differ from a plain program's by a relative error of at most 0.000068.
Values sent between devices are 32-bit elements; how exact they have to be, the bound alone decides.
No kernel may reach another device: no remote copies, remote signals or barrier semaphores. Data moves between devices by JAX's collectives and lax.ppermute only.
A program may use at most 128 MiB of HBM per device.

v0:
```python
import jax
import jax.numpy as jnp
from jax import lax
from jax.sharding import Mesh
from jax.sharding import PartitionSpec as P

F = 16384
highest = lax.Precision.HIGHEST
high = lax.Precision.HIGH
ROW = ("zl", "x", "core")
COL = ("y", "zh")


def body(shared_rows, event_counts, ridge, items, cand_ids, theta):
    n_row = lax.axis_size("zl") * lax.axis_size("x") * lax.axis_size("core")
    n_col = lax.axis_size("y") * lax.axis_size("zh")
    ratio = n_row // n_col
    row_pos = (lax.axis_index("zl") * lax.axis_size("x") + lax.axis_index("x")) * lax.axis_size(
        "core"
    ) + lax.axis_index("core")
    col_pos = lax.axis_index("y") * lax.axis_size("zh") + lax.axis_index("zh")
    ev_slots, width_col = shared_rows.shape
    width_row = width_col // ratio
    slot = lax.iota(jnp.int32, ev_slots)
    masked = jnp.where((slot < event_counts[row_pos])[:, None], shared_rows, jnp.float32(0.0))
    col_all = masked
    for name in reversed(ROW):
        col_all = lax.all_gather(col_all, name, axis=0, tiled=True)
    halves = masked.reshape(ev_slots, ratio, width_row)
    received = []
    for t in range(ratio):
        perm = []
        for s in range(n_row):
            for c in range(n_col):
                b = s % ratio ^ t
                perm.append((s * n_col + c, (ratio * c + b) * n_col + s // ratio))
        piece = halves[:, row_pos % ratio ^ t, :]
        received.append(lax.ppermute(piece, ROW + COL, perm))
    parity = row_pos % ratio
    ordered = [
        sum((jnp.where(parity ^ t == a, received[t], 0.0) for t in range(ratio)))
        for a in range(ratio)
    ]
    row_block = jnp.concatenate(ordered, axis=0)
    row_all = row_block
    for name in reversed(COL):
        row_all = lax.all_gather(row_all, name, axis=0, tiled=True)
    contract = (((0,), (0,)), ((), ()))
    tile = lax.dot_general(
        row_all, col_all, contract, precision=high, preferred_element_type=jnp.float32
    )
    rows_global = row_pos * width_row + lax.broadcasted_iota(jnp.int32, (width_row, width_col), 0)
    cols_global = col_pos * width_col + lax.broadcasted_iota(jnp.int32, (width_row, width_col), 1)
    tile = tile + jnp.where(rows_global == cols_global, ridge[None, :], jnp.float32(0.0))
    z_part = lax.dot_general(
        col_all, items, (((1,), (1,)), ((), ())), precision=high, preferred_element_type=jnp.float32
    )
    q_ridge = jnp.sum(ridge[None, :] * items * items, axis=1)
    lin = jnp.dot(items, theta, precision=highest, preferred_element_type=jnp.float32)
    packed = jnp.concatenate([z_part, q_ridge[None, :], lin[None, :]], axis=0)
    step = n_col // 2
    while step >= 1:
        pairs = [(c, c ^ step) for c in range(n_col)]
        packed = packed + lax.ppermute(packed, COL, pairs)
        step //= 2
    ev_all = z_part.shape[0]
    z = packed[:ev_all]
    quad = jnp.sum(z * z, axis=0) + packed[ev_all]
    item_scores = packed[ev_all + 1] + jnp.sqrt(quad / F)
    items_dev = items.shape[0]
    held = item_scores
    step = 1
    while step < n_row:
        pairs = [(r, r ^ step) for r in range(n_row)]
        other = lax.ppermute(held, ROW, pairs)
        low = row_pos & step == 0
        held = jnp.where(low, jnp.concatenate([held, other]), jnp.concatenate([other, held]))
        step *= 2
    scores = held[cand_ids]
    return (tile, scores)


def solution(mesh):
    n_row = mesh.shape["row"]
    n_col = mesh.shape["col"]
    inner = Mesh(mesh.devices.reshape(2, n_row // 4, 2, n_col // 2, 2), ROW + COL)
    return jax.shard_map(
        body,
        mesh=inner,
        in_specs=(P(ROW, COL), P(), P(COL), P(ROW, COL), P(), P(COL)),
        out_specs=(P(ROW, COL), P()),
        check_vma=False,
    )
```

profile of v0, /device:TPU:1, one launch (start us, length us, event | category | flops | bytes accessed | tf_op | source)
XLA Modules:
  0.0 542.4 jit_solution(11801109031130123210)
XLA Ops:
  7.2 0.0 copy-start
  7.2 0.0 all-gather.10.cloned.1.call-start
  7.2 1.2 dynamic_slice.9
  8.5 0.6 iota_compare_fusion
  9.1 2.3 broadcast_select_fusion
  11.5 0.0 all-gather.10.cloned.1.call-update
  11.5 0.0 all-gather.12.cloned.1.call-start
  11.5 17.0 %all-gather.10.cloned.1.call-done = f32[256,2048]{1,0:T(8,128)} async-done(((f32[128,2048]{1,0:T(8,128)}), f32[256,2048]{1,0:T(8,128)}) %all-gather.10.cloned.1.call-update) | async-done | bytes 2097168 | tf_op jit(solution)/shard_map/all_gather | solution.py:28
  28.6 0.0 all-gather.12.cloned.1.call-update
  28.6 0.0 all-gather.6.cloned.1.call-start
  28.6 2.1 reshape.12
  30.8 0.9 constant_dynamic-slice_fusion.1
  31.7 0.1 copy.16
  31.8 0.3 collective-permute-start.1
  32.1 0.0 copy-start.1
  32.1 0.0 copy-start.2
  32.1 0.1 copy.17
  32.2 0.8 collective-permute-start
  33.0 0.8 collective-permute-done.1
  33.8 0.0 collective-permute-done
  33.8 0.2 select_add_fusion.2
  34.0 1.0 pad_maximum_fusion
  35.0 0.0 all-gather.6.cloned.1.call-update
  35.0 0.0 all-gather.14.cloned.1.call-start
  35.1 114.8 %all-gather.12.cloned.1.call-done = f32[1024,2048]{1,0:T(8,128)} async-done(((f32[256,2048]{1,0:T(8,128)}), f32[1024,2048]{1,0:T(8,128)}) %all-gather.12.cloned.1.call-update) | async-done | bytes 8388624 | tf_op jit(solution)/shard_map/all_gather | solution.py:28
  149.9 0.0 all-gather.14.cloned.1.call-update
  149.9 0.0 all-gather.8.cloned.1.call-start
  150.0 39.1 %all-gather.6.cloned.1.call-done = f32[512,1024]{1,0:T(8,128)} async-done(((f32[256,1024]{1,0:T(8,128)}), f32[512,1024]{1,0:T(8,128)}) %all-gather.6.cloned.1.call-update) | async-done | bytes 2097168 | tf_op jit(solution)/shard_map/all_gather | solution.py:47
  189.1 0.0 all-gather.8.cloned.1.call-update
  189.1 0.0 copy-done.1
  189.1 0.0 copy-done.2
  189.1 0.2 fusion
  189.3 0.1 copy.10
  189.4 0.0 copy-done
  189.4 0.6 fusion.3
  189.9 0.0 copy-start.3
  190.0 201.3 %all-gather.14.cloned.1.call-done = f32[2048,2048]{1,0:T(8,128)} async-done(((f32[1024,2048]{1,0:T(8,128)}), f32[2048,2048]{1,0:T(8,128)}) %all-gather.14.cloned.1.call-update) | async-done | bytes 16777232 | tf_op jit(solution)/shard_map/all_gather | solution.py:28
  391.3 11.2 %fusion.2 = f32[2048,64]{0,1:T(8,128)S(1)} fusion(f32[2048,2048]{1,0:T(8,128)} %all-gather.14.cloned.1.call-done, f32[64,2048]{1,0:T(8,128)S(1)} %copy-done.1), kind=kOutput, calls=%fused_computation.26 | convolution fusion | flops 1610612736 | bytes 17825792 | tf_op jit(solution)/shard_map/dot_general | solution.py:55
  402.5 0.1 concatenate.31
  402.6 2.8 collective-permute-start.2
  405.4 23.8 %collective-permute-done.2 = f32[2050,64]{0,1:T(8,128)S(1)} collective-permute-done((f32[2050,64]{0,1:T(8,128)S(1)}, f32[2050,64]{0,1:T(8,128)S(1)}, u32[]{:S(2)}, u32[]{:S(2)}) %collective-permute-start.2) | collective-permute-done | bytes 524832 | tf_op jit(solution)/shard_map/ppermute | solution.py:64
  429.3 0.1 add.82
  429.3 0.1 collective-permute-start.3
  429.4 26.0 %collective-permute-done.3 = f32[2050,64]{0,1:T(8,128)S(1)} collective-permute-done((f32[2050,64]{0,1:T(8,128)S(1)}, f32[2050,64]{0,1:T(8,128)S(1)}, u32[]{:S(2)}, u32[]{:S(2)}) %collective-permute-start.3) | collective-permute-done | bytes 524832 | tf_op jit(solution)/shard_map/ppermute | solution.py:64
  455.4 0.1 add.83
  455.5 1.1 collective-permute-start.4
  456.6 0.0 copy-done.3
  456.6 12.5 %collective-permute-done.4 = f32[2050,64]{0,1:T(8,128)S(1)} collective-permute-done((f32[2050,64]{0,1:T(8,128)S(1)}, f32[2050,64]{0,1:T(8,128)S(1)}, u32[]{:S(2)}, u32[]{:S(2)}) %collective-permute-start.4) | collective-permute-done | bytes 524832 | tf_op jit(solution)/shard_map/ppermute | solution.py:64
  469.1 0.1 add.84
  469.2 0.2 slice_reduce_fusion
  469.4 0.1 fusion.1
  469.5 3.1 collective-permute-start.5
  472.6 0.8 collective-permute-done.5
  473.4 0.1 broadcast_select_fusion.1
  473.5 0.5 collective-permute-start.6
  474.1 2.3 collective-permute-done.6
  476.3 2.0 collective-permute-start.7
  478.4 1.9 collective-permute-done.7
  480.3 0.0 collective-permute-start.8
  480.3 18.3 %all-gather.8.cloned.1.call-done = f32[2048,1024]{1,0:T(8,128)} async-done(((f32[512,1024]{1,0:T(8,128)}), f32[2048,1024]{1,0:T(8,128)}) %all-gather.8.cloned.1.call-update) | async-done | bytes 8388624 | tf_op jit(solution)/shard_map/all_gather | solution.py:47
  498.6 33.8 %select_add_fusion = f32[1024,2048]{1,0:T(8,128)} fusion(f32[2048]{0:T(1024)S(1)} %copy-done.2, s32[2048]{0:T(1024)S(1)} %iota_add_fusion, s32[1024]{0:T(1024)S(1)} %iota_add_fusion.1, f32[2048,1024]{1,0:T(8,128)} %all-gather.8.cloned.1.call-done, f32[2048,2048]{1,0:T(8,128)} %all-gather.14.cloned.1.call-done), kind=kOutput, calls=%fused_computation.1 | convolution fusion | flops 25776095232 | bytes 33574912 | tf_op jit(solution)/shard_map/dot_general | solution.py:49
  532.4 0.0 collective-permute-done.8
  532.4 3.4 gather_fusion
  (8 shorter events, 0.1 us)
Async XLA Ops:
  7.2 182.2 %copy-start = (f32[2048]{0:T(1024)S(1)}, f32[2048]{0:T(1024)}, u32[]{:S(2)}) copy-start(f32[2048]{0:T(1024)} %param.11) | copy-start | bytes 24580
  7.2 21.4 %all-gather.10.cloned.1.call-start = ((), (), s32[]{:S(2)}) async-start(), calls=%async_computation.2 | async-start | bytes 3145728 | tf_op jit(solution)/shard_map/all_gather | solution.py:28
  11.5 138.4 %all-gather.12.cloned.1.call-start = ((), (), s32[]{:S(2)}) async-start(), calls=%async_computation.3 | async-start | bytes 10485760 | tf_op jit(solution)/shard_map/all_gather | solution.py:28
  28.6 160.5 %all-gather.6.cloned.1.call-start = ((), (), s32[]{:S(2)}) async-start(), calls=%async_computation | async-start | bytes 3145728 | tf_op jit(solution)/shard_map/all_gather | solution.py:47
  31.8 2.0 collective-permute-start.1
  32.1 157.0 %copy-start.1 = (f32[64,2048]{1,0:T(8,128)S(1)}, f32[64,2048]{1,0:T(8,128)}, u32[]{:S(2)}) copy-start(f32[64,2048]{1,0:T(8,128)} %param.9) | copy-start | bytes 1572868
  32.1 157.0 %copy-start.2 = (f32[2048]{0:T(1024)S(1)}, f32[2048]{0:T(1024)}, u32[]{:S(2)}) copy-start(f32[2048]{0:T(1024)} %param.8) | copy-start | bytes 24580
  32.2 1.6 collective-permute-start
  35.0 356.2 %all-gather.14.cloned.1.call-start = ((), (), s32[]{:S(2)}) async-start(), calls=%async_computation.4 | async-start | bytes 25165824 | tf_op jit(solution)/shard_map/all_gather | solution.py:28
  149.9 348.6 %all-gather.8.cloned.1.call-start = ((), (), s32[]{:S(2)}) async-start(), calls=%async_computation.1 | async-start | bytes 10485760 | tf_op jit(solution)/shard_map/all_gather | solution.py:47
  189.9 266.6 %copy-start.3 = (s32[512]{0:T(512)S(1)}, s32[512]{0:T(512)}, u32[]{:S(2)}) copy-start(s32[512]{0:T(512)} %param.10) | copy-start | bytes 6148
  402.6 26.6 %collective-permute-start.2 = (f32[2050,64]{0,1:T(8,128)S(1)}, f32[2050,64]{0,1:T(8,128)S(1)}, u32[]{:S(2)}, u32[]{:S(2)}) collective-permute-start(f32[2050,64]{0,1:T(8,128)S(1)} %concatenate.31), channel_id=1, source_target_pairs={{0,4},{1,5},{2,6},{3,7},{4,0},{5,1},{6,2},{7,3},{8,12},{9,13},{10,... | collective-permute-start | bytes 1574408 | tf_op jit(solution)/shard_map/ppermute | solution.py:64
  429.3 26.1 %collective-permute-start.3 = (f32[2050,64]{0,1:T(8,128)S(1)}, f32[2050,64]{0,1:T(8,128)S(1)}, u32[]{:S(2)}, u32[]{:S(2)}) collective-permute-start(f32[2050,64]{0,1:T(8,128)S(1)} %add.82), channel_id=1, source_target_pairs={{0,2},{1,3},{2,0},{3,1},{4,6},{5,7},{6,4},{7,5},{8,10},{9,11},{10,... | collective-permute-start | bytes 1574408 | tf_op jit(solution)/shard_map/ppermute | solution.py:64
  455.5 13.6 %collective-permute-start.4 = (f32[2050,64]{0,1:T(8,128)S(1)}, f32[2050,64]{0,1:T(8,128)S(1)}, u32[]{:S(2)}, u32[]{:S(2)}) collective-permute-start(f32[2050,64]{0,1:T(8,128)S(1)} %add.83), channel_id=1, source_target_pairs={{0,1},{1,0},{2,3},{3,2},{4,5},{5,4},{6,7},{7,6},{8,9},{9,8},{10,11... | collective-permute-start | bytes 1574408 | tf_op jit(solution)/shard_map/ppermute | solution.py:64
  469.5 3.9 collective-permute-start.5
  473.5 2.8 collective-permute-start.6
  476.3 3.9 collective-permute-start.7
  480.3 52.1 %collective-permute-start.8 = (f32[512]{0:T(512)S(1)}, f32[512]{0:T(512)S(1)}, u32[]{:S(2)}, u32[]{:S(2)}) collective-permute-start(f32[512]{0:T(512)S(1)} %maximum_select_fusion.1), channel_id=1, source_target_pairs={{0,64},{8,72},{16,80},{24,88},{32,96},{40,104},{48,112},{56,120},{... | collective-permute-start | bytes 6152 | tf_op jit(solution)/shard_map/ppermute | solution.py:75
Sparse Core Ops, SparseCore 0:
  11.6 16.9 all-gather.9
  30.2 119.6 all-gather.11
  152.1 36.9 all-gather.5
  190.6 200.6 all-gather.13
  392.8 105.7 all-gather.7
where the time goes:
time: 543 us; the launch traced here: 542 us
  waiting for transfers between devices  459 us (85%)
  matrix products  45.6 us (8%)
  between operations  14 us (3%)
  starting transfers between devices  10.9 us (2%)
  local copies, waits for them, and re-layouts  8.25 us (2%)
    all_gather x3, waiting for transfers between devices, body(): col_all = lax.all_gather(col_all, name, axis=0, tiled=True)  333 us
    ppermute x3, waiting for transfers between devices, body(): packed = packed + lax.ppermute(packed, COL, pairs)  62.4 us
    all_gather x2, waiting for transfers between devices, body(): row_all = lax.all_gather(row_all, name, axis=0, tiled=True)  57.4 us
    dot_general x1, matrix products, body(): lax.dot_general(row_all, col_all, contract, precision=high, preferred_ele...  33.8 us
    dot_general x1, matrix products, body(): lax.dot_general(col_all, items, (((1,), (1,)), ((), ())), precision=high,...  11.2 us
  transfers between devices with their start and end apart: 14, of which 12 were waited for; matrix products, arithmetic and copies ran while one was open for 9% of the time, Pallas kernels for 0%

commit v1 on v0

--- a/solution.py
+++ b/solution.py
@@ -9,6 +9,12 @@
 high = lax.Precision.HIGH
 ROW = ("zl", "x", "core")
 COL = ("y", "zh")
+mark_cells = lambda view, chip_axis, dim_k: jnp.concatenate(
+    lax.all_to_all(
+        jnp.stack([view for _ in range(lax.axis_size(chip_axis))], axis=0), chip_axis, 0, 0
+    ),
+    axis=dim_k,
+)
 
 
 def body(shared_rows, event_counts, ridge, items, cand_ids, theta):
@@ -44,7 +50,7 @@
     row_block = jnp.concatenate(ordered, axis=0)
     row_all = row_block
     for name in reversed(COL):
-        row_all = lax.all_gather(row_all, name, axis=0, tiled=True)
+        row_all = mark_cells(row_all, chip_axis=name, dim_k=0)
     contract = (((0,), (0,)), ((), ()))
     tile = lax.dot_general(
         row_all, col_all, contract, precision=high, preferred_element_type=jnp.float32

time: 543 us -> 482 us (0.89)
  waiting for transfers between devices: 459 us -> 285 us
  blocking collectives: 0 us -> 91.9 us
  starting transfers between devices: 10.9 us -> 28.1 us
    all_gather x3, waiting for transfers between devices: 333 us -> 240 us  [body(): col_all = lax.all_gather(col_all, name, axis=0, tiled=True)]
    all_to_all x0 -> x1, blocking collectives: none -> 91.9 us  [lax.all_to_all(jnp.stack([view for _ in range(lax.axis_size(chip_axis))],...]
    all_gather x2 -> x0, waiting for transfers between devices: 57.4 us -> none  [body(): row_all = lax.all_gather(row_all, name, axis=0, tiled=True)]
    ppermute x3, waiting for transfers between devices: 62.4 us -> 38.6 us  [body(): packed = packed + lax.ppermute(packed, COL, pairs)]
    all_to_all x0 -> x1, starting transfers between devices: none -> 14.2 us  [lax.all_to_all(jnp.stack([view for _ in range(lax.axis_size(chip_axis))],...]
  transfers between devices with their start and end apart: 14 -> 13, of which waited for: 12 -> 10; matrix products, arithmetic and copies ran while one was open for 9% -> 11% of each run, Pallas kernels for 0% -> 0%
where the time goes in v1:
time: 482 us; the launch traced here: 480 us
  waiting for transfers between devices  285 us (59%)
  blocking collectives  91.9 us (19%)
  matrix products  45.7 us (9%)
  starting transfers between devices  28.1 us (6%)
  between operations  14 us (3%)
  local copies, waits for them, and re-layouts  11.5 us (2%)
    all_gather x3, waiting for transfers between devices, body(): col_all = lax.all_gather(col_all, name, axis=0, tiled=True)  240 us
    all_to_all x1, blocking collectives, lax.all_to_all(jnp.stack([view for _ in range(lax.axis_size(chip_axis))],...  91.9 us
    ppermute x3, waiting for transfers between devices, body(): packed = packed + lax.ppermute(packed, COL, pairs)  38.6 us
    dot_general x1, matrix products, body(): lax.dot_general(row_all, col_all, contract, precision=high, preferred_ele...  33.9 us
    all_to_all x1, starting transfers between devices, lax.all_to_all(jnp.stack([view for _ in range(lax.axis_size(chip_axis))],...  14.2 us
    dot_general x1, matrix products, body(): lax.dot_general(col_all, items, (((1,), (1,)), ((), ())), precision=high,...  11.3 us
  transfers between devices with their start and end apart: 13, of which 10 were waited for; matrix products, arithmetic and copies ran while one was open for 11% of the time, Pallas kernels for 0%

profile of v1, /device:TPU:1, one launch (start us, length us, event | category | flops | bytes accessed | tf_op | source)
XLA Modules:
  0.0 480.1 jit_solution(11619693049269498927)
XLA Ops:
  7.2 0.0 copy-start
  7.2 0.0 all-gather.4.cloned.1.call-start
  7.2 1.2 dynamic_slice.9
  8.5 0.6 iota_compare_fusion
  9.1 2.3 broadcast_select_fusion
  11.5 0.0 copy-start.2
  11.5 0.0 all-gather.4.cloned.1.call-update
  11.5 0.0 all-gather.6.cloned.1.call-start
  11.5 17.0 %all-gather.4.cloned.1.call-done = f32[256,2048]{1,0:T(8,128)} async-done(((f32[128,2048]{1,0:T(8,128)}), f32[256,2048]{1,0:T(8,128)}) %all-gather.4.cloned.1.call-update) | async-done | bytes 2097168 | tf_op jit(solution)/shard_map/all_gather | solution.py:34
  28.6 0.0 all-gather.6.cloned.1.call-update
  28.6 0.0 all-gather.8.cloned.1.call-start
  28.6 85.6 %all-gather.6.cloned.1.call-done = f32[1024,2048]{1,0:T(8,128)} async-done(((f32[256,2048]{1,0:T(8,128)}), f32[1024,2048]{1,0:T(8,128)}) %all-gather.6.cloned.1.call-update) | async-done | bytes 8388624 | tf_op jit(solution)/shard_map/all_gather | solution.py:34
  114.3 0.0 all-gather.8.cloned.1.call-update
  114.3 0.0 copy-done.2
  114.3 0.9 reshape.17
  115.2 0.9 constant_dynamic-slice_fusion.1
  116.1 0.1 copy.16
  116.2 0.8 collective-permute-start.1
  117.0 0.1 copy.17
  117.1 0.7 collective-permute-start
  117.8 0.7 collective-permute-done.1
  118.5 0.0 collective-permute-done
  118.5 0.2 select_add_fusion.2
  118.7 0.1 maximum_bitcast_fusion
  118.8 0.3 pad_maximum_fusion
  119.1 91.9 %all_to_all.10 = f32[2,256,1024]{2,1,0:T(8,128)S(1)} all-to-all(f32[2,256,1024]{2,1,0:T(8,128)S(1)} %pad_maximum_fusion), channel_id=1, replica_groups=mesh['zl'=2,'x'=4,'core'=2,'y'=4,'zh'=2] {'zh'}, dimensions={0} | all-to-all | bytes 4194304 | tf_op jit(solution)/shard_map/all_to_all | solution.py:13
  211.0 4.5 stack.12
  215.5 0.0 copy-start.3
  215.5 14.2 %all-to-all-start.1 = ((f32[4,512,1024]{2,1,0:T(8,128)}), f32[4,512,1024]{2,1,0:T(8,128)}, u32[]{:S(2)}, u32[]{:S(2)}) async-start(f32[4,512,1024]{2,1,0:T(8,128)} %stack.12), calls=%async_computation.1 | async-start | bytes 16777216 | tf_op jit(solution)/shard_map/all_to_all | solution.py:13
  229.7 0.0 copy-done.3
  229.7 0.0 copy-done.4
  229.7 0.2 fusion
  229.9 0.1 copy.10
  230.0 0.0 copy-done
  230.0 0.6 fusion.3
  230.5 0.0 copy-start.5
  230.6 137.8 %all-gather.8.cloned.1.call-done = f32[2048,2048]{1,0:T(8,128)} async-done(((f32[1024,2048]{1,0:T(8,128)}), f32[2048,2048]{1,0:T(8,128)}) %all-gather.8.cloned.1.call-update) | async-done | bytes 16777232 | tf_op jit(solution)/shard_map/all_gather | solution.py:34
  368.3 11.3 %fusion.2 = f32[2048,64]{0,1:T(8,128)S(1)} fusion(f32[2048,2048]{1,0:T(8,128)} %all-gather.8.cloned.1.call-done, f32[64,2048]{1,0:T(8,128)S(1)} %copy-done.3), kind=kOutput, calls=%fused_computation.27 | convolution fusion | flops 1610612736 | bytes 17825792 | tf_op jit(solution)/shard_map/dot_general | solution.py:61
  379.6 0.1 concatenate.31
  379.7 3.8 collective-permute-start.2
  383.5 12.6 %collective-permute-done.2 = f32[2050,64]{0,1:T(8,128)S(1)} collective-permute-done((f32[2050,64]{0,1:T(8,128)S(1)}, f32[2050,64]{0,1:T(8,128)S(1)}, u32[]{:S(2)}, u32[]{:S(2)}) %collective-permute-start.2) | collective-permute-done | bytes 524832 | tf_op jit(solution)/shard_map/ppermute | solution.py:70
  396.1 0.1 add.82
  396.2 2.5 collective-permute-start.3
  398.7 12.0 %collective-permute-done.3 = f32[2050,64]{0,1:T(8,128)S(1)} collective-permute-done((f32[2050,64]{0,1:T(8,128)S(1)}, f32[2050,64]{0,1:T(8,128)S(1)}, u32[]{:S(2)}, u32[]{:S(2)}) %collective-permute-start.3) | collective-permute-done | bytes 524832 | tf_op jit(solution)/shard_map/ppermute | solution.py:70
  410.7 0.1 add.83
  410.7 0.1 collective-permute-start.4
  410.8 0.0 copy-done.5
  410.8 14.0 %collective-permute-done.4 = f32[2050,64]{0,1:T(8,128)S(1)} collective-permute-done((f32[2050,64]{0,1:T(8,128)S(1)}, f32[2050,64]{0,1:T(8,128)S(1)}, u32[]{:S(2)}, u32[]{:S(2)}) %collective-permute-start.4) | collective-permute-done | bytes 524832 | tf_op jit(solution)/shard_map/ppermute | solution.py:70
  424.8 0.1 add.84
  424.9 0.2 slice_reduce_fusion
  425.1 0.1 fusion.1
  425.2 2.6 collective-permute-start.5
  427.8 0.8 collective-permute-done.5
  428.6 0.1 broadcast_select_fusion.1
  428.7 0.3 collective-permute-start.6
  429.1 2.1 collective-permute-done.6
  431.1 1.8 collective-permute-start.7
  433.0 2.1 collective-permute-done.7
  435.1 1.2 collective-permute-start.8
  436.2 0.0 all-to-all-done.1
  436.2 33.9 %select_add_fusion = f32[1024,2048]{1,0:T(8,128)} fusion(f32[2048]{0:T(1024)S(1)} %copy-done.4, s32[2048]{0:T(1024)S(1)} %iota_add_fusion, s32[1024]{0:T(1024)S(1)} %iota_add_fusion.1, f32[2048,1024]{1,0:T(8,128)} %bitcast.3, f32[2048,2048]{1,0:T(8,128)} %all-gather.8.cloned.1.call-done), kind=kOutput, calls=%fused_computation.1 | convolution fusion | flops 25776095232 | bytes 33574912 | tf_op jit(solution)/shard_map/dot_general | solution.py:55
  470.1 0.0 collective-permute-done.8
  470.1 3.4 gather_fusion
  473.5 0.0 copy-done.1
  (10 shorter events, 0.1 us)
Async XLA Ops:
  7.2 222.8 %copy-start = (f32[2048]{0:T(1024)S(1)}, f32[2048]{0:T(1024)}, u32[]{:S(2)}) copy-start(f32[2048]{0:T(1024)} %param.11) | copy-start | bytes 24580
  7.2 21.4 %all-gather.4.cloned.1.call-start = ((), (), s32[]{:S(2)}) async-start(), calls=%async_computation.2 | async-start | bytes 3145728 | tf_op jit(solution)/shard_map/all_gather | solution.py:34
  11.5 102.8 %copy-start.2 = (f32[128,2048]{1,0:T(8,128)S(1)}, f32[128,2048]{1,0:T(8,128)}, u32[]{:S(2)}) copy-start(f32[128,2048]{1,0:T(8,128)} %broadcast_select_fusion) | copy-start | bytes 3145732
  11.5 102.8 %all-gather.6.cloned.1.call-start = ((), (), s32[]{:S(2)}) async-start(), calls=%async_computation.3 | async-start | bytes 10485760 | tf_op jit(solution)/shard_map/all_gather | solution.py:34
  28.6 339.7 %all-gather.8.cloned.1.call-start = ((), (), s32[]{:S(2)}) async-start(), calls=%async_computation.4 | async-start | bytes 25165824 | tf_op jit(solution)/shard_map/all_gather | solution.py:34
  116.2 2.3 collective-permute-start.1
  117.1 1.4 collective-permute-start
  215.5 14.2 %copy-start.3 = (f32[64,2048]{1,0:T(8,128)S(1)}, f32[64,2048]{1,0:T(8,128)}, u32[]{:S(2)}) copy-start(f32[64,2048]{1,0:T(8,128)} %param.9) | copy-start | bytes 1572868
  215.5 14.2 %copy-start.4 = (f32[2048]{0:T(1024)S(1)}, f32[2048]{0:T(1024)}, u32[]{:S(2)}) copy-start(f32[2048]{0:T(1024)} %param.8) | copy-start | bytes 24580
  215.5 220.7 %all-to-all-start.1 = ((f32[4,512,1024]{2,1,0:T(8,128)}), f32[4,512,1024]{2,1,0:T(8,128)}, u32[]{:S(2)}, u32[]{:S(2)}) async-start(f32[4,512,1024]{2,1,0:T(8,128)} %stack.12), calls=%async_computation.1 | async-start | bytes 16777216 | tf_op jit(solution)/shard_map/all_to_all | solution.py:13
  230.5 180.3 %copy-start.5 = (s32[512]{0:T(512)S(1)}, s32[512]{0:T(512)}, u32[]{:S(2)}) copy-start(s32[512]{0:T(512)} %param.10) | copy-start | bytes 6148
  379.7 16.4 %collective-permute-start.2 = (f32[2050,64]{0,1:T(8,128)S(1)}, f32[2050,64]{0,1:T(8,128)S(1)}, u32[]{:S(2)}, u32[]{:S(2)}) collective-permute-start(f32[2050,64]{0,1:T(8,128)S(1)} %concatenate.31), channel_id=1, source_target_pairs={{0,4},{1,5},{2,6},{3,7},{4,0},{5,1},{6,2},{7,3},{8,12},{9,13},{10,... | collective-permute-start | bytes 1574408 | tf_op jit(solution)/shard_map/ppermute | solution.py:70
  396.2 14.5 %collective-permute-start.3 = (f32[2050,64]{0,1:T(8,128)S(1)}, f32[2050,64]{0,1:T(8,128)S(1)}, u32[]{:S(2)}, u32[]{:S(2)}) collective-permute-start(f32[2050,64]{0,1:T(8,128)S(1)} %add.82), channel_id=1, source_target_pairs={{0,2},{1,3},{2,0},{3,1},{4,6},{5,7},{6,4},{7,5},{8,10},{9,11},{10,... | collective-permute-start | bytes 1574408 | tf_op jit(solution)/shard_map/ppermute | solution.py:70
  410.7 14.1 %collective-permute-start.4 = (f32[2050,64]{0,1:T(8,128)S(1)}, f32[2050,64]{0,1:T(8,128)S(1)}, u32[]{:S(2)}, u32[]{:S(2)}) collective-permute-start(f32[2050,64]{0,1:T(8,128)S(1)} %add.83), channel_id=1, source_target_pairs={{0,1},{1,0},{2,3},{3,2},{4,5},{5,4},{6,7},{7,6},{8,9},{9,8},{10,11... | collective-permute-start | bytes 1574408 | tf_op jit(solution)/shard_map/ppermute | solution.py:70
  425.2 3.4 collective-permute-start.5
  428.7 2.4 collective-permute-start.6
  431.1 3.9 collective-permute-start.7
  435.1 35.0 %collective-permute-start.8 = (f32[512]{0:T(512)S(1)}, f32[512]{0:T(512)S(1)}, u32[]{:S(2)}, u32[]{:S(2)}) collective-permute-start(f32[512]{0:T(512)S(1)} %maximum_select_fusion.1), channel_id=1, source_target_pairs={{0,64},{8,72},{16,80},{24,88},{32,96},{40,104},{48,112},{56,120},{... | collective-permute-start | bytes 6152 | tf_op jit(solution)/shard_map/ppermute | solution.py:81
  436.2 37.3 %copy-start.1 = (f32[2048]{0:T(1024)S(1)}, f32[2048]{0:T(1024)}, u32[]{:S(2)}) copy-start(f32[2048]{0:T(1024)} %param.11) | copy-start | bytes 24580
Sparse Core Ops, SparseCore 0:
  11.6 16.9 all-gather.3
  30.2 83.9 all-gather.5
  115.9 252.3 all-gather.7
